TPU v7x, 32 devices: a whole 2x2x4 slice. The times are simulated.
32 devices in a mesh: fsdp: 4 (over x, core), replica: 8 (over z, y).
Axes of the slice: x: 2, y: 2, z: 4, core: 2. Of those that a mesh axis runs over, the one named last changes fastest.
Arguments:
- hidden_in: bfloat16 [16384, 768], P(('fsdp', 'replica')), may hold values from -6 to 6
- encoder_states: bfloat16 [16384, 768], P(('fsdp', 'replica')), may hold values from -6 to 6
- output_grad: bfloat16 [16384, 768], P(('fsdp', 'replica')), may hold values from -6 to 6
- piece_starts: int32 [32, 3], P(('fsdp', 'replica')), may hold values from 0 to 384, as said below
- selfquery: bfloat16 [768, 768], P('fsdp'), may hold values from -0.0546875 to 0.0546875
- selfkey: bfloat16 [768, 768], P('fsdp'), may hold values from -0.21875 to 0.21875
- selfvalue: bfloat16 [768, 768], P('fsdp'), may hold values from -0.21875 to 0.21875
- selfproj: bfloat16 [768, 768], P('fsdp'), may hold values from -0.875 to 0.875
- crossquery: bfloat16 [768, 768], P('fsdp'), may hold values from -0.0546875 to 0.0546875
- crosskey: bfloat16 [768, 768], P('fsdp'), may hold values from -0.21875 to 0.21875
- crossvalue: bfloat16 [768, 768], P('fsdp'), may hold values from -0.21875 to 0.21875
- crossproj: bfloat16 [768, 768], P('fsdp'), may hold values from -0.875 to 0.875
- gateproj: bfloat16 [768, 2048], P('fsdp'), may hold values from -0.21875 to 0.21875
- upproj: bfloat16 [768, 2048], P('fsdp'), may hold values from -0.21875 to 0.21875
- downproj: bfloat16 [2048, 768], P('fsdp'), may hold values from -0.125 to 0.125
- gainself: bfloat16 [768], P('fsdp'), may hold values from 0.5 to 1.5
- gaincross: bfloat16 [768], P('fsdp'), may hold values from 0.5 to 1.5
- gainffn: bfloat16 [768], P('fsdp'), may hold values from 0.5 to 1.5
- reltable: bfloat16 [32, 12], P('fsdp'), may hold values from -4 to 4
Outputs:
- layer_out: bfloat16 [16384, 768], P(('fsdp', 'replica'))
- hidden_grad: float32 [16384, 768], P(('fsdp', 'replica'))
- encoder_grad: float32 [16384, 768], P(('fsdp', 'replica'))
- selfquery_grad: float32 [768, 768], P('fsdp')
- selfkey_grad: float32 [768, 768], P('fsdp')
- selfvalue_grad: float32 [768, 768], P('fsdp')
- selfproj_grad: float32 [768, 768], P('fsdp')
- crossquery_grad: float32 [768, 768], P('fsdp')
- crosskey_grad: float32 [768, 768], P('fsdp')
- crossvalue_grad: float32 [768, 768], P('fsdp')
- crossproj_grad: float32 [768, 768], P('fsdp')
- gateproj_grad: float32 [768, 2048], P('fsdp')
- upproj_grad: float32 [768, 2048], P('fsdp')
- downproj_grad: float32 [2048, 768], P('fsdp')
- gainself_grad: float32 [768], P('fsdp')
- gaincross_grad: float32 [768], P('fsdp')
- gainffn_grad: float32 [768], P('fsdp')
- reltable_grad: float32 [32, 12], P('fsdp')
Inputs may be any that keep to these rules, and one draw needn't show every extreme that they name: `piece_starts`: each row holds the 3 increasing starts of one sequence's pieces, the first 0 and the last exactly 384; no piece has more than 256 tokens, and each sequence has one piece of exactly 256.
All inputs are finite; a program needn't handle non-finite values.
Results may differ from a plain program's by a relative error of at most 0.028.
The roundings to bfloat16 on the way count: a program that leaves them out, or rounds other values in their place, can miss the bound.
Values may be sent and summed in bfloat16 or wider, within the bound.
No kernel may reach another device: no remote copies, remote signals or barrier semaphores. Data moves between devices by JAX's collectives and lax.ppermute only.
A program may use at most 256 MiB of HBM per device.

v0:
```python
import jax
import jax.numpy as jnp
from jax import lax
from jax.sharding import PartitionSpec as P

HEADS = 12
HEAD_DIM = 64
BUCKETS = 32
QBLOCK = 512
EPS = 1e-06
NEG = -1000000000.0
EDGES = (1, 2, 3, 4, 5, 6, 7, 8, 12, 16, 23, 32, 46, 64, 91)


def rms_scale(hidden, gain):
    return hidden * lax.rsqrt(jnp.mean(hidden * hidden, axis=-1, keepdims=True) + EPS) * gain


def gated(gate, upper):
    return jax.nn.gelu(gate, approximate=True) * upper


def product(left, right):
    return jnp.dot(left, right, preferred_element_type=jnp.float32)


def left_product(left, right):
    return lax.dot_general(
        left, right, (((0,), (0,)), ((), ())), preferred_element_type=jnp.float32
    )


def right_product(left, right):
    return lax.dot_general(
        left, right, (((1,), (1,)), ((), ())), preferred_element_type=jnp.float32
    )


def split_heads(matrix):
    return matrix.reshape(matrix.shape[0], HEADS, HEAD_DIM)


def block_terms(context, block_rows, key_count):
    if context is None:
        return (None, None, None)
    rel_table, piece_ids = context
    query_pos = jnp.arange(block_rows, dtype=jnp.int32)
    key_pos = jnp.arange(key_count, dtype=jnp.int32)
    relative = key_pos[None, :] - query_pos[:, None]
    distance = jnp.abs(relative)
    bucket = 16 * (relative > 0).astype(jnp.int32)
    for edge_len in EDGES:
        bucket = bucket + (distance >= edge_len).astype(jnp.int32)
    onehot = (bucket[:, :, None] == jnp.arange(BUCKETS, dtype=jnp.int32)[None, None, :]).astype(
        jnp.bfloat16
    )
    bias_block = jnp.einsum("qkb,bh->hqk", onehot, rel_table, preferred_element_type=jnp.float32)
    allowed = (key_pos[None, :] <= query_pos[:, None]) | (piece_ids[None, :] == piece_ids[:, None])
    return (onehot, bias_block, allowed)


def block_scores(query_block, key_heads, bias_block, allowed):
    scores = jnp.einsum("qhd,khd->hqk", query_block, key_heads, preferred_element_type=jnp.float32)
    if bias_block is not None:
        scores = jnp.where(allowed[None], scores + bias_block, NEG)
    return scores


def attend_forward(queries, key_rows, value_rows, context):
    key_heads = split_heads(key_rows)
    value_heads = split_heads(value_rows)
    query_block = split_heads(queries)
    onehot, bias_block, allowed = block_terms(context, QBLOCK, key_rows.shape[0])
    scores = block_scores(query_block, key_heads, bias_block, allowed)
    row_max = jnp.max(scores, axis=-1, keepdims=True)
    raised = jnp.exp(scores - row_max)
    row_sum = jnp.sum(raised, axis=-1, keepdims=True)
    prob_low = (raised / row_sum).astype(jnp.bfloat16)
    mixed_block = jnp.einsum(
        "hqk,khd->qhd", prob_low, value_heads, preferred_element_type=jnp.float32
    )
    mixed_parts = mixed_block.reshape(QBLOCK, HEADS * HEAD_DIM).astype(jnp.bfloat16)
    lse_parts = row_max + jnp.log(row_sum)
    return (mixed_parts, lse_parts)


def attend_backward(queries, key_rows, value_rows, grad_mixed, lse_rows, context):
    key_count = key_rows.shape[0]
    key_heads = split_heads(key_rows)
    value_heads = split_heads(value_rows)
    table_grad = jnp.zeros((BUCKETS, HEADS), jnp.float32)
    query_block = split_heads(queries)
    grad_block = split_heads(grad_mixed)
    onehot, bias_block, allowed = block_terms(context, QBLOCK, key_count)
    scores = block_scores(query_block, key_heads, bias_block, allowed)
    probs = jnp.exp(scores - lse_rows)
    prob_low = probs.astype(jnp.bfloat16)
    grad_probs = jnp.einsum(
        "qhd,khd->hqk", grad_block, value_heads, preferred_element_type=jnp.float32
    )
    inner_sum = jnp.sum(probs * grad_probs, axis=-1, keepdims=True)
    grad_scores = (probs * (grad_probs - inner_sum)).astype(jnp.bfloat16)
    query_grad = jnp.einsum(
        "hqk,khd->qhd", grad_scores, key_heads, preferred_element_type=jnp.float32
    )
    query_parts = query_grad.reshape(QBLOCK, HEADS * HEAD_DIM).astype(jnp.bfloat16)
    key_grad = jnp.einsum(
        "hqk,qhd->khd", grad_scores, query_block, preferred_element_type=jnp.float32
    )
    value_grad = jnp.einsum(
        "hqk,qhd->khd", prob_low, grad_block, preferred_element_type=jnp.float32
    )
    if onehot is not None:
        table_grad = jnp.einsum(
            "hqk,qkb->bh", grad_scores, onehot, preferred_element_type=jnp.float32
        )
    key_low = key_grad.reshape(key_count, HEADS * HEAD_DIM).astype(jnp.bfloat16)
    value_low = value_grad.reshape(key_count, HEADS * HEAD_DIM).astype(jnp.bfloat16)
    return (query_parts, key_low, value_low, table_grad)


def make_on_device(fsdp_size, replica_size):

    def on_device(
        hidden_in,
        encoder_states,
        output_grad,
        piece_starts,
        selfquery,
        selfkey,
        selfvalue,
        selfproj,
        crossquery,
        crosskey,
        crossvalue,
        crossproj,
        gateproj,
        upproj,
        downproj,
        gainself,
        gaincross,
        gainffn,
        reltable,
    ):
        shard_rows, width = selfquery.shape
        ff_width = gateproj.shape[1]
        table_rows = reltable.shape[0]
        self_packed = jnp.concatenate([selfquery, selfkey, selfvalue], axis=1)
        small_packed = jnp.concatenate([gainself, gaincross, gainffn, reltable.reshape(-1)])
        mid_packed = jnp.concatenate(
            [selfproj, crossquery, crosskey, crossvalue, crossproj], axis=1
        )
        ffn_packed = jnp.concatenate([gateproj, upproj, downproj.reshape(shard_rows, -1)], axis=1)
        self_full = lax.all_gather(self_packed, "fsdp", axis=0, tiled=True)
        small_full = lax.all_gather(small_packed, "fsdp", axis=0, tiled=False)
        mid_full = lax.all_gather(mid_packed, "fsdp", axis=0, tiled=True)
        ffn_full = lax.all_gather(ffn_packed, "fsdp", axis=0, tiled=True)
        gain_one = small_full[:, 0:shard_rows].reshape(-1)
        gain_two = small_full[:, shard_rows : 2 * shard_rows].reshape(-1)
        gain_three = small_full[:, 2 * shard_rows : 3 * shard_rows].reshape(-1)
        table_full = small_full[:, 3 * shard_rows :].reshape(-1, HEADS)
        self_proj = mid_full[:, 0:width]
        cross_query = mid_full[:, width : 2 * width]
        cross_kv = mid_full[:, 2 * width : 4 * width]
        cross_key = cross_kv[:, :width]
        cross_value = cross_kv[:, width:]
        cross_proj = mid_full[:, 4 * width : 5 * width]
        gate_up = ffn_full[:, : 2 * ff_width]
        down_full = (
            ffn_full[:, 2 * ff_width :]
            .reshape(fsdp_size, shard_rows, ff_width)
            .reshape(ff_width, width)
        )
        length = hidden_in.shape[0]
        position = jnp.arange(length, dtype=jnp.int32)
        piece_ids = (
            jnp.sum((piece_starts[0][None, :] <= position[:, None]).astype(jnp.int32), axis=1) - 1
        )
        context = (table_full, piece_ids)
        resid_in = hidden_in.astype(jnp.float32)
        normed_one = rms_scale(resid_in, gain_one.astype(jnp.float32)).astype(jnp.bfloat16)
        qkv_one = product(normed_one, self_full).astype(jnp.bfloat16)
        query_one = qkv_one[:, :width]
        key_one = qkv_one[:, width : 2 * width]
        value_one = qkv_one[:, 2 * width :]
        mixed_one, lse_one = attend_forward(query_one, key_one, value_one, context)
        after_self = resid_in + product(mixed_one, self_proj)
        normed_two = rms_scale(after_self, gain_two.astype(jnp.float32)).astype(jnp.bfloat16)
        query_two = product(normed_two, cross_query).astype(jnp.bfloat16)
        kv_two = product(encoder_states, cross_kv).astype(jnp.bfloat16)
        key_two = kv_two[:, :width]
        value_two = kv_two[:, width:]
        mixed_two, lse_two = attend_forward(query_two, key_two, value_two, None)
        after_cross = after_self + product(mixed_two, cross_proj)
        normed_three = rms_scale(after_cross, gain_three.astype(jnp.float32)).astype(jnp.bfloat16)
        gate_upper = product(normed_three, gate_up)
        gate_pre = gate_upper[:, :ff_width]
        upper_pre = gate_upper[:, ff_width:]
        inner = gated(gate_pre, upper_pre).astype(jnp.bfloat16)
        layer_out = (after_cross + product(inner, down_full)).astype(jnp.bfloat16)

        def reduce_rows(packed):
            owned = lax.psum_scatter(
                packed.astype(jnp.bfloat16), ("fsdp", "replica"), scatter_dimension=0, tiled=True
            )
            return lax.all_gather(owned, "replica", axis=0, tiled=True)

        downproj_grad = left_product(inner, output_grad)
        inner_grad = right_product(output_grad, down_full)
        gated_value, pull_gate = jax.vjp(gated, gate_pre, upper_pre)
        gate_grad, upper_grad = pull_gate(inner_grad)
        gate_upper_low = jnp.concatenate(
            [gate_grad.astype(jnp.bfloat16), upper_grad.astype(jnp.bfloat16)], axis=1
        )
        gate_up_grad = left_product(normed_three, gate_upper_low)
        ffn_owned = reduce_rows(
            jnp.concatenate([gate_up_grad, downproj_grad.reshape(width, ff_width)], axis=1)
        )
        normed_grad = right_product(gate_upper_low, gate_up)
        norm_value, pull_norm = jax.vjp(rms_scale, after_cross, gain_three.astype(jnp.float32))
        back_resid, gainffn_grad = pull_norm(normed_grad)
        resid_grad = output_grad.astype(jnp.float32) + back_resid
        branch_low = resid_grad.astype(jnp.bfloat16)
        crossproj_grad = left_product(mixed_two, branch_low)
        mixed_grad = right_product(branch_low, cross_proj).astype(jnp.bfloat16)
        query_back, key_back, value_back, unused_table = attend_backward(
            query_two, key_two, value_two, mixed_grad, lse_two, None
        )
        crossquery_grad = left_product(normed_two, query_back)
        kv_back = jnp.concatenate([key_back, value_back], axis=1)
        crosskv_grad = left_product(encoder_states, kv_back)
        cross_owned = reduce_rows(
            jnp.concatenate([crossproj_grad, crossquery_grad, crosskv_grad], axis=1)
        )
        encoder_grad = right_product(kv_back, cross_kv)
        normed_grad = right_product(query_back, cross_query)
        norm_value, pull_norm = jax.vjp(rms_scale, after_self, gain_two.astype(jnp.float32))
        back_resid, gaincross_grad = pull_norm(normed_grad)
        resid_grad = resid_grad + back_resid
        branch_low = resid_grad.astype(jnp.bfloat16)
        selfproj_grad = left_product(mixed_one, branch_low)
        mixed_grad = right_product(branch_low, self_proj).astype(jnp.bfloat16)
        query_back, key_back, value_back, reltable_grad = attend_backward(
            query_one, key_one, value_one, mixed_grad, lse_one, context
        )
        qkv_back = jnp.concatenate([query_back, key_back, value_back], axis=1)
        selfqkv_grad = left_product(normed_one, qkv_back)
        self_owned = reduce_rows(jnp.concatenate([selfproj_grad, selfqkv_grad], axis=1))
        normed_grad = right_product(qkv_back, self_full)
        norm_value, pull_norm = jax.vjp(rms_scale, resid_in, gain_one.astype(jnp.float32))
        back_resid, gainself_grad = pull_norm(normed_grad)
        hidden_grad = resid_grad + back_resid
        small_sum = lax.psum(
            jnp.concatenate(
                [gainself_grad, gaincross_grad, gainffn_grad, reltable_grad.reshape(-1)]
            ),
            ("fsdp", "replica"),
        )
        me = lax.axis_index("fsdp")
        gain_block = lambda i: lax.dynamic_slice_in_dim(
            small_sum, i * width + me * shard_rows, shard_rows
        )
        table_block = lax.dynamic_slice_in_dim(
            small_sum[3 * width :].reshape(-1, HEADS), me * table_rows, table_rows
        )
        as_f32 = lambda v: v.astype(jnp.float32)
        return (
            layer_out,
            hidden_grad,
            encoder_grad,
            as_f32(self_owned[:, width : 2 * width]),
            as_f32(self_owned[:, 2 * width : 3 * width]),
            as_f32(self_owned[:, 3 * width : 4 * width]),
            as_f32(self_owned[:, 0:width]),
            as_f32(cross_owned[:, width : 2 * width]),
            as_f32(cross_owned[:, 2 * width : 3 * width]),
            as_f32(cross_owned[:, 3 * width : 4 * width]),
            as_f32(cross_owned[:, 0:width]),
            as_f32(ffn_owned[:, 0:ff_width]),
            as_f32(ffn_owned[:, ff_width : 2 * ff_width]),
            as_f32(ffn_owned[:, 2 * ff_width :].reshape(-1, width)),
            gain_block(0),
            gain_block(1),
            gain_block(2),
            table_block,
        )

    return on_device


def solution(mesh):
    placed = (
        P(("fsdp", "replica"), None),
        P(("fsdp", "replica"), None),
        P(("fsdp", "replica"), None),
        P(("fsdp", "replica"), None),
        P("fsdp", None),
        P("fsdp", None),
        P("fsdp", None),
        P("fsdp", None),
        P("fsdp", None),
        P("fsdp", None),
        P("fsdp", None),
        P("fsdp", None),
        P("fsdp", None),
        P("fsdp", None),
        P("fsdp", None),
        P("fsdp"),
        P("fsdp"),
        P("fsdp"),
        P("fsdp", None),
    )
    return jax.shard_map(
        make_on_device(mesh.shape["fsdp"], mesh.shape["replica"]),
        mesh=mesh,
        in_specs=placed,
        out_specs=(
            P(("fsdp", "replica"), None),
            P(("fsdp", "replica"), None),
            P(("fsdp", "replica"), None),
            P("fsdp", None),
            P("fsdp", None),
            P("fsdp", None),
            P("fsdp", None),
            P("fsdp", None),
            P("fsdp", None),
            P("fsdp", None),
            P("fsdp", None),
            P("fsdp", None),
            P("fsdp", None),
            P("fsdp", None),
            P("fsdp"),
            P("fsdp"),
            P("fsdp"),
            P("fsdp", None),
        ),
        check_vma=False,
    )
```

profile of v0, /device:TPU:0, one launch (start us, length us, event | category | flops | bytes accessed | tf_op | source)
XLA Modules:
  0.0 753.6 jit_solution(3771571763767273229)
XLA Ops:
  21.4 9.3 %all-reduce = bf16[2688]{0:T(1024)(128)(2,1)S(1)} all-reduce(bf16[2688]{0:T(1024)(128)(2,1)S(1)} %dynamic-update-slice), channel_id=2, replica_groups=mesh['fsdp'=4,'replica'=8] {'fsdp'}, use_global_device_ids=true, to_apply=%add | all-reduce | flops 2688 | bytes 10752
  31.9 8.7 %iota_compare_fusion = pred[512,512,32]{0,2,1:T(32,128)(4,1)} fusion(s32[512,512]{0,1:T(8,128)S(1)} %convert_add_fusion.1), kind=kLoop, calls=%fused_computation | loop fusion | flops 8388608 | bytes 9437184 | tf_op jit(solution)/shard_map/eq | solution.py:54
  40.5 46.2 %copy.117 = pred[512,512,32]{1,2,0:T(32,128)(4,1)S(1)} copy(pred[512,512,32]{0,2,1:T(32,128)(4,1)} %iota_compare_fusion) | data formatting | bytes 16777216 | tf_op jit(solution)/shard_map/eq | solution.py:54
  86.8 7.7 %fusion.83 = f32[12,512,512]{2,0,1:T(8,128)} fusion(pred[512,512,32]{1,2,0:T(32,128)(4,1)S(1)} %copy.117, bf16[32,12]{1,0:T(8,128)(2,1)S(1)} %reshape.325), kind=kOutput, calls=%fused_computation.155 | convolution fusion | flops 201326592 | bytes 20972288 | tf_op jit(solution)/shard_map/qkb,bh->hqk/dot_general | solution.py:57
  94.5 18.3 %copy.118 = f32[12,512,512]{1,2,0:T(8,128)} copy(f32[12,512,512]{2,0,1:T(8,128)} %fusion.83) | data formatting | bytes 25165824 | tf_op jit(solution)/shard_map/qkb,bh->hqk/dot_general | solution.py:57
  113.6 4.1 convolution_convert_fusion.2
  121.1 6.6 fusion.97
  161.9 3.9 slice.140
  165.8 6.6 reshape_reshape.3
  172.4 10.2 %fusion.16 = f32[512,4096]{1,0:T(8,128)} fusion(bf16[768,6144]{1,0:T(8,128)(2,1)} %all-gather.12.cloned.1.call-done, f32[512,768]{1,0:T(8,128)} %get-tuple-element.92, f32[768]{0:T(1024)S(1)} %reshape.337, f32[512]{0:T(512)S(1)} %fusion.87), kind=kOutput, calls=%fused_computation.30 | convolution fusion | flops 3222405120 | bytes 16258048 | tf_op jit(solution)/shard_map/dot_general | solution.py:24
  182.7 8.4 %fusion.24 = (bf16[512,2048]{1,0:T(8,128)(2,1)S(1)}, bf16[512,2048]{1,0:T(8,128)(2,1)S(1)}, bf16[512,2048]{1,0:T(8,128)(2,1)}) fusion(f32[512,4096]{1,0:T(8,128)} %fusion.16, bf16[2048,768]{1,0:T(8,128)(2,1)S(1)} %copy-done.28, bf16[512,768]{1,0:T(8,128)(2,1)S(1)} %copy-done.42), kind=kOutput, calls=%fused_computation.42 | convolution fusion | flops 1637875712 | bytes 18612224 | tf_op jit(solution)/shard_map/dot_general | solution.py:34
  191.2 3.7 multiply_reduce_fusion.2
  203.2 7.9 %fusion.40 = bf16[12,64,512]{2,1,0:T(8,128)(2,1)} fusion(bf16[512,12,64]{0,2,1:T(8,128)(2,1)} %bitcast.98, f32[12,512,512]{1,2,0:T(8,128)} %copy-done.2, f32[12,512]{1,0:T(8,128)S(1)} %log_add_fusion.1), kind=kOutput, calls=%fused_computation.93 | convolution fusion | flops 409337856 | bytes 14180352 | tf_op jit(solution)/shard_map/hqk,qhd->khd/dot_general | solution.py:110
  211.1 9.0 %multiply_reduce_fusion.1 = (f32[12,512]{1,0:T(8,128)S(1)}, f32[12,512,512]{1,2,0:T(8,128)}) fusion(f32[12,512,512]{1,2,0:T(8,128)} %copy-done.2, f32[12,512]{1,0:T(8,128)S(1)} %log_add_fusion.1, bf16[512,12,64]{0,2,1:T(8,128)(2,1)S(1)} %bitcast.99, bf16[512,12,64]{0,2,1:T(8,128)(2,1)S(1)} %bitcast.109), kind=kOutput, calls=%fused_computation.5 | convolution fusion | flops 412084224 | bytes 26787840 | tf_op jit(solution)/shard_map/qhd,khd->hqk/dot_general | solution.py:98
  220.1 7.4 multiply_convert_fusion.1
  235.9 6.6 copy.148
  257.0 12.8 %multiply_reduce_fusion = (f32[12,512]{1,0:T(8,128)S(1)}, f32[12,512,512]{1,2,0:T(8,128)}) fusion(f32[12,512,512]{1,2,0:T(8,128)} %copy-done.1, f32[12,512]{1,0:T(8,128)S(1)} %log_add_fusion, bf16[512,12,64]{0,2,1:T(8,128)(2,1)} %bitcast.96, bf16[512,12,64]{0,2,1:T(8,128)(2,1)} %bitcast.107), kind=kOutput, calls=%fused_computation.2 | convolution fusion | flops 412084224 | bytes 26787840 | tf_op jit(solution)/shard_map/qhd,khd->hqk/dot_general | solution.py:98
  269.8 7.1 multiply_convert_fusion
  289.3 5.0 convolution_convert_fusion.3
  294.4 6.6 reshape.332
  301.0 6.4 convolution_convert_fusion
  307.4 4.2 pad_maximum_fusion
  311.7 39.2 %reduce-scatter.10.cloned.1.call-done = bf16[24,3072]{1,0:T(8,128)(2,1)} async-done(((bf16[768,3072]{1,0:T(8,128)(2,1)}), bf16[24,3072]{1,0:T(8,128)(2,1)}) %reduce-scatter.10.cloned.1.call-update) | async-done | bytes 147472 | tf_op jit(solution)/shard_map/reduce_scatter | solution.py:203
  351.0 111.8 %reduce-scatter.6.cloned.1.call-done = bf16[24,3072]{1,0:T(8,128)(2,1)} async-done(((bf16[768,3072]{1,0:T(8,128)(2,1)}), bf16[24,3072]{1,0:T(8,128)(2,1)}) %reduce-scatter.6.cloned.1.call-update) | async-done | bytes 147472 | tf_op jit(solution)/shard_map/reduce_scatter | solution.py:203
  462.8 141.1 %reduce-scatter.8.cloned.1.call-done = bf16[24,6144]{1,0:T(8,128)(2,1)} async-done(((bf16[768,6144]{1,0:T(8,128)(2,1)}), bf16[24,6144]{1,0:T(8,128)(2,1)}) %reduce-scatter.8.cloned.1.call-update) | async-done | bytes 294928 | tf_op jit(solution)/shard_map/reduce_scatter | solution.py:203
  604.0 8.5 %fusion.48 = f32[32,12]{1,0:T(8,128)S(1)} fusion(bf16[12,512,512]{1,2,0:T(8,128)(2,1)} %copy-done.3, s32[512,512]{0,1:T(8,128)S(1)} %copy-done.22), kind=kOutput, calls=%fused_computation.101 | convolution fusion | flops 209715200 | bytes 7341568 | tf_op jit(solution)/shard_map/hqk,qkb->bh/dot_general | solution.py:114
  612.6 6.4 fusion.34
  619.0 40.8 %psum.7 = f32[2688]{0:T(1024)S(1)} all-reduce(f32[2688]{0:T(1024)S(1)} %pad_maximum_fusion.14), channel_id=1, replica_groups=mesh['fsdp'=4,'replica'=8] {'fsdp','replica'}, use_global_device_ids=true, to_apply=%region_19.20 | all-reduce | flops 2688 | bytes 21504 | tf_op jit(solution)/shard_map/psum | solution.py:253
  664.2 4.4 fusion.28
  674.0 14.6 %all-gather.14.cloned.1.call-done = bf16[192,3072]{1,0:T(8,128)(2,1)} async-done(((bf16[24,3072]{1,0:T(8,128)(2,1)}), bf16[192,3072]{1,0:T(8,128)(2,1)}) %all-gather.14.cloned.1.call-update) | async-done | bytes 1179664 | tf_op jit(solution)/shard_map/all_gather | solution.py:206
  691.3 50.1 %all-gather.18.cloned.1.call-done = bf16[192,6144]{1,0:T(8,128)(2,1)} async-done(((bf16[24,6144]{1,0:T(8,128)(2,1)}), bf16[192,6144]{1,0:T(8,128)(2,1)}) %all-gather.18.cloned.1.call-update) | async-done | bytes 2359312 | tf_op jit(solution)/shard_map/all_gather | solution.py:206
  741.3 3.9 slice_convert_fusion
  (244 shorter events, 110.3 us)
Async XLA Ops:
  7.2 137.0 %copy-start = (bf16[512,768]{1,0:T(8,128)(2,1)S(1)}, bf16[512,768]{1,0:T(8,128)(2,1)}, u32[]{:S(2)}) copy-start(bf16[512,768]{1,0:T(8,128)(2,1)} %param.20) | copy-start | bytes 2359300
  7.2 106.2 %all-gather.8.cloned.1.call-start = ((), (), s32[]{:S(2)}) async-start(), calls=%async_computation.3 | async-start | bytes 4423680 | tf_op jit(solution)/shard_map/all_gather | solution.py:154
  9.5 126.0 %all-gather.10.cloned.1.call-start = ((), (), s32[]{:S(2)}) async-start(), calls=%async_computation.4 | async-start | bytes 7372800 | tf_op jit(solution)/shard_map/all_gather | solution.py:156
  14.7 147.2 %all-gather.12.cloned.1.call-start = ((), (), s32[]{:S(2)}) async-start(), calls=%async_computation.5 | async-start | bytes 11796480 | tf_op jit(solution)/shard_map/all_gather | solution.py:157
  19.7 331.3 %reduce-scatter.10.cloned.1.call-start = ((), (), s32[]{:S(2)}) async-start(), calls=%async_computation.11 | async-start | bytes 4866048 | tf_op jit(solution)/shard_map/reduce_scatter | solution.py:203
  31.1 82.2 %copy-start.50 = (f32[768]{0:T(1024)}, f32[768]{0:T(1024)S(1)}, u32[]{:S(2)}) copy-start(f32[768]{0:T(1024)S(1)} %reshape.335) | copy-start | bytes 9220
  31.8 8.7 %copy-start.21 = (s32[512,512]{0,1:T(8,128)}, s32[512,512]{0,1:T(8,128)S(1)}, u32[]{:S(2)}) copy-start(s32[512,512]{0,1:T(8,128)S(1)} %convert_add_fusion.1) | copy-start | bytes 3145732
  94.5 18.3 %copy-start.55 = (s32[1,3]{1,0:T(1,128)S(1)}, s32[1,3]{1,0:T(1,128)}, u32[]{:S(2)}) copy-start(s32[1,3]{1,0:T(1,128)} %param.22) | copy-start | bytes 40
  94.5 18.4 %copy-start.30 = (bf16[512,768]{1,0:T(8,128)(2,1)S(1)}, bf16[512,768]{1,0:T(8,128)(2,1)}, u32[]{:S(2)}) copy-start(bf16[512,768]{1,0:T(8,128)(2,1)} %param.19) | copy-start | bytes 2359300
  119.3 8.3 %copy-start.14 = (bf16[512,768]{0,1:T(8,128)(2,1)}, bf16[512,768]{0,1:T(8,128)(2,1)S(1)}, u32[]{:S(2)}) copy-start(bf16[512,768]{0,1:T(8,128)(2,1)S(1)} %copy.114) | copy-start | bytes 2359300
  121.1 8.5 %copy-start.23 = (bf16[512,768]{0,1:T(8,128)(2,1)}, bf16[512,768]{0,1:T(8,128)(2,1)S(1)}, u32[]{:S(2)}) copy-start(bf16[512,768]{0,1:T(8,128)(2,1)S(1)} %copy.113) | copy-start | bytes 2359300
  138.3 104.4 %copy-start.6 = (f32[512,768]{1,0:T(8,128)}, f32[512,768]{1,0:T(8,128)S(1)}, u32[]{:S(2)}) copy-start(f32[512,768]{1,0:T(8,128)S(1)} %get-tuple-element.88) | copy-start | bytes 4718596
  172.4 10.2 %copy-start.28 = (bf16[2048,768]{1,0:T(8,128)(2,1)S(1)}, bf16[2048,768]{1,0:T(8,128)(2,1)}, u32[]{:S(2)}) copy-start(bf16[2048,768]{1,0:T(8,128)(2,1)} %reshape_reshape.3) | copy-start | bytes 9437188
  172.4 10.2 %copy-start.42 = (bf16[512,768]{1,0:T(8,128)(2,1)S(1)}, bf16[512,768]{1,0:T(8,128)(2,1)}, u32[]{:S(2)}) copy-start(bf16[512,768]{1,0:T(8,128)(2,1)} %param.21) | copy-start | bytes 2359300
  172.4 18.7 %slice-start.6 = ((s8[9437184]{0:T(1024)(128)(4,1)}), s8[4194304]{0:T(1024)(128)(4,1)S(1)}, s32[]{:S(2)}) async-start(s8[9437184]{0:T(1024)(128)(4,1)} %bitcast.114), calls=%async_computation.18 | async-start | bytes 8388608
  182.6 8.5 %copy-start.7 = (f32[512,768]{1,0:T(8,128)S(1)}, f32[512,768]{1,0:T(8,128)}, u32[]{:S(2)}) copy-start(f32[512,768]{1,0:T(8,128)} %get-tuple-element.92) | copy-start | bytes 4718596
  182.7 8.5 %slice-start.7 = ((s8[9437184]{0:T(1024)(128)(4,1)}), s8[4194304]{0:T(1024)(128)(4,1)S(1)}, s32[]{:S(2)}) async-start(s8[9437184]{0:T(1024)(128)(4,1)} %bitcast.114), calls=%async_computation.19 | async-start | bytes 8388608
  182.7 8.5 %slice-start.8 = ((s8[9437184]{0:T(1024)(128)(4,1)}), s8[1048576]{0:T(1024)(128)(4,1)S(1)}, s32[]{:S(2)}) async-start(s8[9437184]{0:T(1024)(128)(4,1)} %bitcast.114), calls=%async_computation.20 | async-start | bytes 2097152
  203.2 16.9 %slice-start.3 = ((s8[12582912]{0:T(1024)(128)(4,1)}), s8[4194304]{0:T(1024)(128)(4,1)S(1)}, s32[]{:S(2)}) async-start(s8[12582912]{0:T(1024)(128)(4,1)} %bitcast.90), calls=%async_computation.15 | async-start | bytes 8388608
  203.2 16.9 %slice-start.4 = ((s8[12582912]{0:T(1024)(128)(4,1)}), s8[4194304]{0:T(1024)(128)(4,1)S(1)}, s32[]{:S(2)}) async-start(s8[12582912]{0:T(1024)(128)(4,1)} %bitcast.90), calls=%async_computation.16 | async-start | bytes 8388608
  211.1 9.0 %slice-start.5 = ((s8[12582912]{0:T(1024)(128)(4,1)}), s8[4194304]{0:T(1024)(128)(4,1)S(1)}, s32[]{:S(2)}) async-start(s8[12582912]{0:T(1024)(128)(4,1)} %bitcast.90), calls=%async_computation.17 | async-start | bytes 8388608
  242.5 220.2 %reduce-scatter.6.cloned.1.call-start = ((), (), s32[]{:S(2)}) async-start(), calls=%async_computation.6 | async-start | bytes 4866048 | tf_op jit(solution)/shard_map/reduce_scatter | solution.py:203
  257.0 12.8 %slice-start = ((s8[12582912]{0:T(1024)(128)(4,1)}), s8[4194304]{0:T(1024)(128)(4,1)S(1)}, s32[]{:S(2)}) async-start(s8[12582912]{0:T(1024)(128)(4,1)} %bitcast.88), calls=%async_computation.12 | async-start | bytes 8388608
  257.0 12.8 %slice-start.1 = ((s8[12582912]{0:T(1024)(128)(4,1)}), s8[4194304]{0:T(1024)(128)(4,1)S(1)}, s32[]{:S(2)}) async-start(s8[12582912]{0:T(1024)(128)(4,1)} %bitcast.88), calls=%async_computation.13 | async-start | bytes 8388608
  257.0 12.8 %slice-start.2 = ((s8[12582912]{0:T(1024)(128)(4,1)}), s8[4194304]{0:T(1024)(128)(4,1)S(1)}, s32[]{:S(2)}) async-start(s8[12582912]{0:T(1024)(128)(4,1)} %bitcast.88), calls=%async_computation.14 | async-start | bytes 8388608
  288.2 315.8 %reduce-scatter.8.cloned.1.call-start = ((), (), s32[]{:S(2)}) async-start(), calls=%async_computation.9 | async-start | bytes 9732096 | tf_op jit(solution)/shard_map/reduce_scatter | solution.py:203
  311.6 292.4 %copy-start.22 = (s32[512,512]{0,1:T(8,128)S(1)}, s32[512,512]{0,1:T(8,128)}, u32[]{:S(2)}) copy-start(s32[512,512]{0,1:T(8,128)} %copy-done.21) | copy-start | bytes 3145732
  311.6 359.7 %all-gather.16.cloned.1.call-start = ((), (), s32[]{:S(2)}) async-start(), calls=%async_computation.8 | async-start | bytes 1327104 | tf_op jit(solution)/shard_map/all_gather | solution.py:206
  351.0 337.6 %all-gather.14.cloned.1.call-start = ((), (), s32[]{:S(2)}) async-start(), calls=%async_computation.7 | async-start | bytes 1327104 | tf_op jit(solution)/shard_map/all_gather | solution.py:206
  462.8 278.5 %all-gather.18.cloned.1.call-start = ((), (), s32[]{:S(2)}) async-start(), calls=%async_computation.10 | async-start | bytes 2654208 | tf_op jit(solution)/shard_map/all_gather | solution.py:206
  612.6 48.6 %copy-start.49 = (f32[512]{0:T(512)S(1)}, f32[512]{0:T(512)}, u32[]{:S(2)}) copy-start(f32[512]{0:T(512)} %copy-done.48) | copy-start | bytes 6148
  612.6 48.6 %copy-start.32 = (bf16[512,768]{1,0:T(8,128)(2,1)S(1)}, bf16[512,768]{1,0:T(8,128)(2,1)}, u32[]{:S(2)}) copy-start(bf16[512,768]{1,0:T(8,128)(2,1)} %param.19) | copy-start | bytes 2359300
  (47 other events, 158.8 us)
Sparse Core Ops, SparseCore 0:
  10.2 33.7 all-gather.7
  46.1 44.1 all-gather.9
  91.8 64.2 all-gather.11
  242.7 108.2 reduce-scatter.9
  356.3 106.4 reduce-scatter.5
  468.5 135.4 reduce-scatter.7
  606.2 40.2 all-gather.15
  648.6 39.9 all-gather.13
  690.8 50.4 all-gather.17
where the time goes:
time: 762 us; the launch traced here: 754 us
  waiting for transfers between devices  357 us (47%)
  matrix products  149 us (20%)
  local copies, waits for them, and re-layouts  124 us (16%)
  other arithmetic  57.1 us (7%)
  blocking collectives  50.1 us (7%)
  between operations  15.8 us (2%)
    reduce_scatter x3, waiting for transfers between devices, reduce_rows(): lax.psum_scatter(packed.astype(jnp.bfloat16), ('fsdp', 'replica'), scatte...  292 us
    all_gather x3, waiting for transfers between devices, reduce_rows(): return lax.all_gather(owned, 'replica', axis=0, tiled=True)  64.7 us
    eq x1, local copies, waits for them, and re-layouts, block_terms(): bucket[:, :, None] == jnp.arange(BUCKETS, dtype=jnp.int32)[None, None, :]  46.2 us
    psum x1, blocking collectives, on_device(): lax.psum(jnp.concatenate([gainself_grad, gaincross_grad, gainffn_grad, re...  40.8 us
    dot_general x7, matrix products, right_product(): lax.dot_general(left, right, (((1,), (1,)), ((), ())), preferred_element_...  31.6 us
    dot_general x7, matrix products, product(): return jnp.dot(left, right, preferred_element_type=jnp.float32)  29.6 us
    dot_general x2, matrix products, attend_backward(): jnp.einsum('qhd,khd->hqk', grad_block, value_heads, preferred_element_typ...  21.8 us
    unnamed x148, local copies, waits for them, and re-layouts  21.7 us
  transfers between devices with their start and end apart: 9, of which 5 were waited for; matrix products, arithmetic and copies ran while one was open for 31% of the time, Pallas kernels for 0%

commit v1 on v0

--- a/solution.py
+++ b/solution.py
@@ -10,6 +10,24 @@
 EPS = 1e-06
 NEG = -1000000000.0
 EDGES = (1, 2, 3, 4, 5, 6, 7, 8, 12, 16, 23, 32, 46, 64, 91)
+
+
+def collect(array, axis, dim):
+    ways, here, step = (lax.axis_size(axis), lax.axis_index(axis), array.shape[dim])
+    dims = [n * ways if d == dim else n for d, n in enumerate(array.shape)]
+    full = lax.dynamic_update_slice_in_dim(
+        jnp.zeros(dims, array.dtype), array, here * step, axis=dim
+    )
+    going_up = going_down = array
+    for far in range(1, ways // 2 + 1):
+        going_up = lax.ppermute(going_up, axis, [(d, (d + 1) % ways) for d in range(ways)])
+        full = lax.dynamic_update_slice_in_dim(full, going_up, (here - far) % ways * step, axis=dim)
+        if 2 * far < ways:
+            going_down = lax.ppermute(going_down, axis, [(d, (d - 1) % ways) for d in range(ways)])
+            full = lax.dynamic_update_slice_in_dim(
+                full, going_down, (here + far) % ways * step, axis=dim
+            )
+    return full
 
 
 def rms_scale(hidden, gain):
@@ -203,7 +221,7 @@
             owned = lax.psum_scatter(
                 packed.astype(jnp.bfloat16), ("fsdp", "replica"), scatter_dimension=0, tiled=True
             )
-            return lax.all_gather(owned, "replica", axis=0, tiled=True)
+            return collect(owned, "replica", 0)
 
         downproj_grad = left_product(inner, output_grad)
         inner_grad = right_product(output_grad, down_full)

time: 762 us -> 675 us (0.89)
  waiting for transfers between devices: 357 us -> 232 us
  starting transfers between devices: 0.58 us -> 43.3 us
    reduce_scatter x3, waiting for transfers between devices: 292 us -> 173 us  [reduce_rows(): lax.psum_scatter(packed.astype(jnp.bfloat16), ('fsdp', 'replica'), scatte...]
    all_gather x3 -> x0, waiting for transfers between devices: 64.7 us -> none  [reduce_rows(): return lax.all_gather(owned, 'replica', axis=0, tiled=True)]
    ppermute x0 -> x21, waiting for transfers between devices: none -> 58.5 us  [the longest x12 47.7 us: collect(): lax.ppermute(going_up, axis, [(d, (d + 1) % ways) for d in range(ways)])]
    ppermute x0 -> x21, starting transfers between devices: none -> 42.8 us  [the longest x9 26.6 us: collect(): lax.ppermute(going_down, axis, [(d, (d - 1) % ways) for d in range(ways)])]
    unnamed x148 -> x158, local copies, waits for them, and re-layouts: 21.7 us -> 20.6 us
  transfers between devices with their start and end apart: 9 -> 27, of which waited for: 5 -> 12; matrix products, arithmetic and copies ran while one was open for 31% -> 34% of each run, Pallas kernels for 0% -> 0%
where the time goes in v1:
time: 675 us; the launch traced here: 667 us
  waiting for transfers between devices  232 us (34%)
  matrix products  150 us (22%)
  local copies, waits for them, and re-layouts  123 us (18%)
  other arithmetic  53 us (8%)
  blocking collectives  49.1 us (7%)
  starting transfers between devices  43.3 us (6%)
  between operations  16.4 us (2%)
    reduce_scatter x3, waiting for transfers between devices, reduce_rows(): lax.psum_scatter(packed.astype(jnp.bfloat16), ('fsdp', 'replica'), scatte...  173 us
    ppermute x12, waiting for transfers between devices, collect(): lax.ppermute(going_up, axis, [(d, (d + 1) % ways) for d in range(ways)])  47.7 us
    eq x1, local copies, waits for them, and re-layouts, block_terms(): bucket[:, :, None] == jnp.arange(BUCKETS, dtype=jnp.int32)[None, None, :]  45.9 us
    psum x1, blocking collectives, on_device(): lax.psum(jnp.concatenate([gainself_grad, gaincross_grad, gainffn_grad, re...  39.9 us
    dot_general x7, matrix products, right_product(): lax.dot_general(left, right, (((1,), (1,)), ((), ())), preferred_element_...  31.5 us
    dot_general x7, matrix products, product(): return jnp.dot(left, right, preferred_element_type=jnp.float32)  29.9 us
    ppermute x9, starting transfers between devices, collect(): lax.ppermute(going_down, axis, [(d, (d - 1) % ways) for d in range(ways)])  26.6 us
    dot_general x2, matrix products, attend_backward(): jnp.einsum('qhd,khd->hqk', grad_block, value_heads, preferred_element_typ...  21.8 us
  transfers between devices with their start and end apart: 27, of which 12 were waited for; matrix products, arithmetic and copies ran while one was open for 34% of the time, Pallas kernels for 0%

profile of v1, /device:TPU:0, one launch (start us, length us, event | category | flops | bytes accessed | tf_op | source)
XLA Modules:
  0.0 666.6 jit_solution(7170786070298802272)
XLA Ops:
  19.1 9.2 %all-reduce = bf16[2688]{0:T(1024)(128)(2,1)S(1)} all-reduce(bf16[2688]{0:T(1024)(128)(2,1)S(1)} %dynamic-update-slice), channel_id=2, replica_groups=mesh['fsdp'=4,'replica'=8] {'fsdp'}, use_global_device_ids=true, to_apply=%add | all-reduce | flops 2688 | bytes 10752
  29.5 8.7 %iota_compare_fusion = pred[512,512,32]{0,2,1:T(32,128)(4,1)} fusion(s32[512,512]{0,1:T(8,128)S(1)} %convert_add_fusion.1), kind=kLoop, calls=%fused_computation | loop fusion | flops 8388608 | bytes 9437184 | tf_op jit(solution)/shard_map/eq | solution.py:72
  38.3 45.9 %copy.127 = pred[512,512,32]{1,2,0:T(32,128)(4,1)S(1)} copy(pred[512,512,32]{0,2,1:T(32,128)(4,1)} %iota_compare_fusion) | data formatting | bytes 16777216 | tf_op jit(solution)/shard_map/eq | solution.py:72
  84.2 7.7 %fusion.83 = f32[12,512,512]{2,0,1:T(8,128)} fusion(pred[512,512,32]{1,2,0:T(32,128)(4,1)S(1)} %copy.127, bf16[32,12]{1,0:T(8,128)(2,1)S(1)} %reshape.325), kind=kOutput, calls=%fused_computation.155 | convolution fusion | flops 201326592 | bytes 20972288 | tf_op jit(solution)/shard_map/qkb,bh->hqk/dot_general | solution.py:75
  91.8 18.2 %copy.128 = f32[12,512,512]{1,2,0:T(8,128)} copy(f32[12,512,512]{2,0,1:T(8,128)} %fusion.83) | data formatting | bytes 25165824 | tf_op jit(solution)/shard_map/qkb,bh->hqk/dot_general | solution.py:75
  110.9 4.1 convolution_convert_fusion.2
  118.4 6.5 fusion.97
  162.8 6.6 reshape_reshape.3
  169.4 10.2 %fusion.16 = f32[512,4096]{1,0:T(8,128)} fusion(bf16[768,6144]{1,0:T(8,128)(2,1)} %all-gather.9.cloned.1.call-done, f32[512,768]{1,0:T(8,128)} %get-tuple-element.56, f32[768]{0:T(1024)S(1)} %reshape.337, f32[512]{0:T(512)S(1)} %fusion.87), kind=kOutput, calls=%fused_computation.30 | convolution fusion | flops 3222405120 | bytes 16258048 | tf_op jit(solution)/shard_map/dot_general | solution.py:42
  179.7 8.3 %fusion.24 = (bf16[512,2048]{1,0:T(8,128)(2,1)S(1)}, bf16[512,2048]{1,0:T(8,128)(2,1)S(1)}, bf16[512,2048]{1,0:T(8,128)(2,1)}) fusion(f32[512,4096]{1,0:T(8,128)} %fusion.16, bf16[2048,768]{1,0:T(8,128)(2,1)S(1)} %copy-done.28, bf16[512,768]{1,0:T(8,128)(2,1)S(1)} %copy-done.42), kind=kOutput, calls=%fused_computation.42 | convolution fusion | flops 1637875712 | bytes 18612224 | tf_op jit(solution)/shard_map/dot_general | solution.py:52
  200.1 7.9 %fusion.40 = bf16[12,64,512]{2,1,0:T(8,128)(2,1)} fusion(bf16[512,12,64]{0,2,1:T(8,128)(2,1)} %bitcast.98, f32[12,512,512]{1,2,0:T(8,128)} %copy-done.2, f32[12,512]{1,0:T(8,128)S(1)} %log_add_fusion.1), kind=kOutput, calls=%fused_computation.93 | convolution fusion | flops 409337856 | bytes 14180352 | tf_op jit(solution)/shard_map/hqk,qhd->khd/dot_general | solution.py:128
  208.0 9.0 %multiply_reduce_fusion.1 = (f32[12,512]{1,0:T(8,128)S(1)}, f32[12,512,512]{1,2,0:T(8,128)}) fusion(f32[12,512,512]{1,2,0:T(8,128)} %copy-done.2, f32[12,512]{1,0:T(8,128)S(1)} %log_add_fusion.1, bf16[512,12,64]{0,2,1:T(8,128)(2,1)S(1)} %bitcast.99, bf16[512,12,64]{0,2,1:T(8,128)(2,1)S(1)} %bitcast.109), kind=kOutput, calls=%fused_computation.5 | convolution fusion | flops 412084224 | bytes 26787840 | tf_op jit(solution)/shard_map/qhd,khd->hqk/dot_general | solution.py:116
  217.0 7.1 %multiply_convert_fusion.1 = bf16[12,512,512]{1,2,0:T(8,128)(2,1)S(1)} fusion(f32[12,512,512]{1,2,0:T(8,128)} %get-tuple-element.59, f32[12,512,512]{1,2,0:T(8,128)S(1)} %bitcast.91, f32[12,512]{1,0:T(8,128)S(1)} %get-tuple-element.58, f32[12,512]{1,0:T(8,128)S(1)} %log_add_fusion.1), kind=kLoop, calls=%fused_computation.4 | loop fusion | flops 12582912 | bytes 31506432 | tf_op jit(solution)/shard_map/convert_element_type | solution.py:120
  232.6 6.6 copy.160
  253.9 12.8 %multiply_reduce_fusion = (f32[12,512]{1,0:T(8,128)S(1)}, f32[12,512,512]{1,2,0:T(8,128)}) fusion(f32[12,512,512]{1,2,0:T(8,128)} %copy-done.1, f32[12,512]{1,0:T(8,128)S(1)} %log_add_fusion, bf16[512,12,64]{0,2,1:T(8,128)(2,1)} %bitcast.96, bf16[512,12,64]{0,2,1:T(8,128)(2,1)} %bitcast.107), kind=kOutput, calls=%fused_computation.2 | convolution fusion | flops 412084224 | bytes 26787840 | tf_op jit(solution)/shard_map/qhd,khd->hqk/dot_general | solution.py:116
  266.8 7.1 %multiply_convert_fusion = bf16[12,512,512]{1,2,0:T(8,128)(2,1)S(1)} fusion(f32[12,512,512]{1,2,0:T(8,128)} %get-tuple-element.62, f32[12,512,512]{1,2,0:T(8,128)S(1)} %bitcast.89, f32[12,512]{1,0:T(8,128)S(1)} %get-tuple-element.61, f32[12,512]{1,0:T(8,128)S(1)} %log_add_fusion), kind=kLoop, calls=%fused_computation.1 | loop fusion | flops 12582912 | bytes 31506432 | tf_op jit(solution)/shard_map/convert_element_type | solution.py:120
  286.3 5.1 convolution_convert_fusion.3
  291.4 6.6 reshape.332
  298.0 6.4 convolution_convert_fusion
  304.4 4.2 pad_maximum_fusion
  309.8 8.5 %fusion.48 = f32[32,12]{1,0:T(8,128)S(1)} fusion(bf16[12,512,512]{1,2,0:T(8,128)(2,1)} %copy-done.3, s32[512,512]{0,1:T(8,128)S(1)} %copy-done.22), kind=kOutput, calls=%fused_computation.101 | convolution fusion | flops 209715200 | bytes 7341568 | tf_op jit(solution)/shard_map/hqk,qkb->bh/dot_general | solution.py:132
  318.4 6.4 fusion.34
  324.8 39.9 %psum.7 = f32[2688]{0:T(1024)S(1)} all-reduce(f32[2688]{0:T(1024)S(1)} %pad_maximum_fusion.14), channel_id=1, replica_groups=mesh['fsdp'=4,'replica'=8] {'fsdp','replica'}, use_global_device_ids=true, to_apply=%region_19.20 | all-reduce | flops 2688 | bytes 21504 | tf_op jit(solution)/shard_map/psum | solution.py:271
  369.3 4.4 fusion.28
  381.2 77.9 %reduce-scatter.6.cloned.1.call-done = bf16[24,3072]{1,0:T(8,128)(2,1)} async-done(((bf16[768,3072]{1,0:T(8,128)(2,1)}), bf16[24,3072]{1,0:T(8,128)(2,1)}) %reduce-scatter.6.cloned.1.call-update) | async-done | bytes 147472 | tf_op jit(solution)/shard_map/reduce_scatter | solution.py:221
  468.3 6.1 collective-permute-start.3
  504.9 95.1 %reduce-scatter.8.cloned.1.call-done = bf16[24,6144]{1,0:T(8,128)(2,1)} async-done(((bf16[768,6144]{1,0:T(8,128)(2,1)}), bf16[24,6144]{1,0:T(8,128)(2,1)}) %reduce-scatter.8.cloned.1.call-update) | async-done | bytes 294928 | tf_op jit(solution)/shard_map/reduce_scatter | solution.py:221
  603.4 10.7 %collective-permute-done.15 = bf16[24,6144]{1,0:T(8,128)(2,1)S(1)} collective-permute-done((bf16[24,6144]{1,0:T(8,128)(2,1)}, bf16[24,6144]{1,0:T(8,128)(2,1)S(1)}, u32[]{:S(2)}, u32[]{:S(2)}) %collective-permute-start.15) | collective-permute-done | bytes 294944 | tf_op jit(solution)/shard_map/ppermute | solution.py:26
  614.9 5.0 collective-permute-done.14
  624.7 10.3 %collective-permute-done.16 = bf16[24,6144]{1,0:T(8,128)(2,1)S(1)} collective-permute-done((bf16[24,6144]{1,0:T(8,128)(2,1)S(1)}, bf16[24,6144]{1,0:T(8,128)(2,1)S(1)}, u32[]{:S(2)}, u32[]{:S(2)}) %collective-permute-start.16) | collective-permute-done | bytes 294944 | tf_op jit(solution)/shard_map/ppermute | solution.py:23
  637.5 8.2 %collective-permute-done.18 = bf16[24,6144]{1,0:T(8,128)(2,1)S(1)} collective-permute-done((bf16[24,6144]{1,0:T(8,128)(2,1)S(1)}, bf16[24,6144]{1,0:T(8,128)(2,1)S(1)}, u32[]{:S(2)}, u32[]{:S(2)}) %collective-permute-start.18) | collective-permute-done | bytes 294944 | tf_op jit(solution)/shard_map/ppermute | solution.py:23
  645.9 9.8 %collective-permute-done.20 = bf16[24,6144]{1,0:T(8,128)(2,1)S(1)} collective-permute-done((bf16[24,6144]{1,0:T(8,128)(2,1)S(1)}, bf16[24,6144]{1,0:T(8,128)(2,1)S(1)}, u32[]{:S(2)}, u32[]{:S(2)}) %collective-permute-start.20) | collective-permute-done | bytes 294944 | tf_op jit(solution)/shard_map/ppermute | solution.py:23
  (313 shorter events, 169.5 us)
Async XLA Ops:
  7.2 134.3 %copy-start = (bf16[512,768]{1,0:T(8,128)(2,1)S(1)}, bf16[512,768]{1,0:T(8,128)(2,1)}, u32[]{:S(2)}) copy-start(bf16[512,768]{1,0:T(8,128)(2,1)} %param.20) | copy-start | bytes 2359300
  7.2 103.4 %all-gather.5.cloned.1.call-start = ((), (), s32[]{:S(2)}) async-start(), calls=%async_computation.3 | async-start | bytes 4423680 | tf_op jit(solution)/shard_map/all_gather | solution.py:172
  9.5 123.3 %all-gather.7.cloned.1.call-start = ((), (), s32[]{:S(2)}) async-start(), calls=%async_computation.4 | async-start | bytes 7372800 | tf_op jit(solution)/shard_map/all_gather | solution.py:174
  11.9 146.9 %all-gather.9.cloned.1.call-start = ((), (), s32[]{:S(2)}) async-start(), calls=%async_computation.5 | async-start | bytes 11796480 | tf_op jit(solution)/shard_map/all_gather | solution.py:175
  16.9 359.6 %reduce-scatter.10.cloned.1.call-start = ((), (), s32[]{:S(2)}) async-start(), calls=%async_computation.8 | async-start | bytes 4866048 | tf_op jit(solution)/shard_map/reduce_scatter | solution.py:221
  28.8 81.8 %copy-start.55 = (f32[768]{0:T(1024)}, f32[768]{0:T(1024)S(1)}, u32[]{:S(2)}) copy-start(f32[768]{0:T(1024)S(1)} %reshape.335) | copy-start | bytes 9220
  135.5 103.8 %copy-start.6 = (f32[512,768]{1,0:T(8,128)}, f32[512,768]{1,0:T(8,128)S(1)}, u32[]{:S(2)}) copy-start(f32[512,768]{1,0:T(8,128)S(1)} %get-tuple-element.52) | copy-start | bytes 4718596
  239.2 219.8 %reduce-scatter.6.cloned.1.call-start = ((), (), s32[]{:S(2)}) async-start(), calls=%async_computation.6 | async-start | bytes 4866048 | tf_op jit(solution)/shard_map/reduce_scatter | solution.py:221
  285.2 314.8 %reduce-scatter.8.cloned.1.call-start = ((), (), s32[]{:S(2)}) async-start(), calls=%async_computation.7 | async-start | bytes 9732096 | tf_op jit(solution)/shard_map/reduce_scatter | solution.py:221
  318.4 47.7 %copy-start.54 = (f32[512]{0:T(512)S(1)}, f32[512]{0:T(512)}, u32[]{:S(2)}) copy-start(f32[512]{0:T(512)} %copy-done.53) | copy-start | bytes 6148
  318.4 47.7 %copy-start.32 = (bf16[512,768]{1,0:T(8,128)(2,1)S(1)}, bf16[512,768]{1,0:T(8,128)(2,1)}, u32[]{:S(2)}) copy-start(bf16[512,768]{1,0:T(8,128)(2,1)} %param.19) | copy-start | bytes 2359300
  376.5 87.0 %collective-permute-start.7 = (bf16[24,3072]{1,0:T(8,128)(2,1)}, bf16[24,3072]{1,0:T(8,128)(2,1)S(1)}, u32[]{:S(2)}, u32[]{:S(2)}) collective-permute-start(bf16[24,3072]{1,0:T(8,128)(2,1)} %reduce-scatter.10.cloned.1.call-done), channel_id=1, source_target_pairs={{0,1},{1,2},{2,3},{3,4},{4,5},{5,6},{6,7},{7,0},{8,9},{9,10},{10,1... | collective-permute-start | bytes 442376 | tf_op jit(solution)/shard_map/ppermute | solution.py:23
  378.7 86.0 %collective-permute-start.8 = (bf16[24,3072]{1,0:T(8,128)(2,1)}, bf16[24,3072]{1,0:T(8,128)(2,1)S(1)}, u32[]{:S(2)}, u32[]{:S(2)}) collective-permute-start(bf16[24,3072]{1,0:T(8,128)(2,1)} %reduce-scatter.10.cloned.1.call-done), channel_id=1, source_target_pairs={{0,7},{1,0},{2,1},{3,2},{4,3},{5,4},{6,5},{7,6},{8,15},{9,8},{10,9... | collective-permute-start | bytes 442376 | tf_op jit(solution)/shard_map/ppermute | solution.py:26
  459.1 9.2 %collective-permute-start.1 = (bf16[24,3072]{1,0:T(8,128)(2,1)}, bf16[24,3072]{1,0:T(8,128)(2,1)S(1)}, u32[]{:S(2)}, u32[]{:S(2)}) collective-permute-start(bf16[24,3072]{1,0:T(8,128)(2,1)} %reduce-scatter.6.cloned.1.call-done), channel_id=1, source_target_pairs={{0,7},{1,0},{2,1},{3,2},{4,3},{5,4},{6,5},{7,6},{8,15},{9,8},{10,9... | collective-permute-start | bytes 442376 | tf_op jit(solution)/shard_map/ppermute | solution.py:26
  462.2 12.2 %collective-permute-start = (bf16[24,3072]{1,0:T(8,128)(2,1)}, bf16[24,3072]{1,0:T(8,128)(2,1)S(1)}, u32[]{:S(2)}, u32[]{:S(2)}) collective-permute-start(bf16[24,3072]{1,0:T(8,128)(2,1)} %reduce-scatter.6.cloned.1.call-done), channel_id=1, source_target_pairs={{0,1},{1,2},{2,3},{3,4},{4,5},{5,6},{6,7},{7,0},{8,9},{9,10},{10,1... | collective-permute-start | bytes 442376 | tf_op jit(solution)/shard_map/ppermute | solution.py:23
  463.5 15.0 %collective-permute-start.9 = (bf16[24,3072]{1,0:T(8,128)(2,1)S(1)}, bf16[24,3072]{1,0:T(8,128)(2,1)S(1)}, u32[]{:S(2)}, u32[]{:S(2)}) collective-permute-start(bf16[24,3072]{1,0:T(8,128)(2,1)S(1)} %collective-permute-done.7), channel_id=1, source_target_pairs={{0,1},{1,2},{2,3},{3,4},{4,5},{5,6},{6,7},{7,0},{8,9},{9,10},{10,1... | collective-permute-start | bytes 442376 | tf_op jit(solution)/shard_map/ppermute | solution.py:23
  464.8 16.4 %collective-permute-start.10 = (bf16[24,3072]{1,0:T(8,128)(2,1)S(1)}, bf16[24,3072]{1,0:T(8,128)(2,1)S(1)}, u32[]{:S(2)}, u32[]{:S(2)}) collective-permute-start(bf16[24,3072]{1,0:T(8,128)(2,1)S(1)} %collective-permute-done.8), channel_id=1, source_target_pairs={{0,7},{1,0},{2,1},{3,2},{4,3},{5,4},{6,5},{7,6},{8,15},{9,8},{10,9... | collective-permute-start | bytes 442376 | tf_op jit(solution)/shard_map/ppermute | solution.py:26
  468.3 14.9 %collective-permute-start.3 = (bf16[24,3072]{1,0:T(8,128)(2,1)S(1)}, bf16[24,3072]{1,0:T(8,128)(2,1)S(1)}, u32[]{:S(2)}, u32[]{:S(2)}) collective-permute-start(bf16[24,3072]{1,0:T(8,128)(2,1)S(1)} %collective-permute-done.1), channel_id=1, source_target_pairs={{0,7},{1,0},{2,1},{3,2},{4,3},{5,4},{6,5},{7,6},{8,15},{9,8},{10,9... | collective-permute-start | bytes 442376 | tf_op jit(solution)/shard_map/ppermute | solution.py:26
  474.4 12.0 %collective-permute-start.2 = (bf16[24,3072]{1,0:T(8,128)(2,1)S(1)}, bf16[24,3072]{1,0:T(8,128)(2,1)S(1)}, u32[]{:S(2)}, u32[]{:S(2)}) collective-permute-start(bf16[24,3072]{1,0:T(8,128)(2,1)S(1)} %collective-permute-done), channel_id=1, source_target_pairs={{0,1},{1,2},{2,3},{3,4},{4,5},{5,6},{6,7},{7,0},{8,9},{9,10},{10,1... | collective-permute-start | bytes 442376 | tf_op jit(solution)/shard_map/ppermute | solution.py:23
  478.5 11.2 %collective-permute-start.11 = (bf16[24,3072]{1,0:T(8,128)(2,1)S(1)}, bf16[24,3072]{1,0:T(8,128)(2,1)S(1)}, u32[]{:S(2)}, u32[]{:S(2)}) collective-permute-start(bf16[24,3072]{1,0:T(8,128)(2,1)S(1)} %collective-permute-done.9), channel_id=1, source_target_pairs={{0,1},{1,2},{2,3},{3,4},{4,5},{5,6},{6,7},{7,0},{8,9},{9,10},{10,1... | collective-permute-start | bytes 442376 | tf_op jit(solution)/shard_map/ppermute | solution.py:23
  481.1 14.3 %collective-permute-start.12 = (bf16[24,3072]{1,0:T(8,128)(2,1)S(1)}, bf16[24,3072]{1,0:T(8,128)(2,1)S(1)}, u32[]{:S(2)}, u32[]{:S(2)}) collective-permute-start(bf16[24,3072]{1,0:T(8,128)(2,1)S(1)} %collective-permute-done.10), channel_id=1, source_target_pairs={{0,7},{1,0},{2,1},{3,2},{4,3},{5,4},{6,5},{7,6},{8,15},{9,8},{10,9... | collective-permute-start | bytes 442376 | tf_op jit(solution)/shard_map/ppermute | solution.py:26
  483.2 12.2 %collective-permute-start.5 = (bf16[24,3072]{1,0:T(8,128)(2,1)S(1)}, bf16[24,3072]{1,0:T(8,128)(2,1)S(1)}, u32[]{:S(2)}, u32[]{:S(2)}) collective-permute-start(bf16[24,3072]{1,0:T(8,128)(2,1)S(1)} %collective-permute-done.3), channel_id=1, source_target_pairs={{0,7},{1,0},{2,1},{3,2},{4,3},{5,4},{6,5},{7,6},{8,15},{9,8},{10,9... | collective-permute-start | bytes 442376 | tf_op jit(solution)/shard_map/ppermute | solution.py:26
  486.4 7.8 %collective-permute-start.4 = (bf16[24,3072]{1,0:T(8,128)(2,1)S(1)}, bf16[24,3072]{1,0:T(8,128)(2,1)S(1)}, u32[]{:S(2)}, u32[]{:S(2)}) collective-permute-start(bf16[24,3072]{1,0:T(8,128)(2,1)S(1)} %collective-permute-done.2), channel_id=1, source_target_pairs={{0,1},{1,2},{2,3},{3,4},{4,5},{5,6},{6,7},{7,0},{8,9},{9,10},{10,1... | collective-permute-start | bytes 442376 | tf_op jit(solution)/shard_map/ppermute | solution.py:23
  489.7 9.3 %collective-permute-start.13 = (bf16[24,3072]{1,0:T(8,128)(2,1)S(1)}, bf16[24,3072]{1,0:T(8,128)(2,1)S(1)}, u32[]{:S(2)}, u32[]{:S(2)}) collective-permute-start(bf16[24,3072]{1,0:T(8,128)(2,1)S(1)} %collective-permute-done.11), channel_id=1, source_target_pairs={{0,1},{1,2},{2,3},{3,4},{4,5},{5,6},{6,7},{7,0},{8,9},{9,10},{10,1... | collective-permute-start | bytes 442376 | tf_op jit(solution)/shard_map/ppermute | solution.py:23
  494.2 7.8 %collective-permute-start.6 = (bf16[24,3072]{1,0:T(8,128)(2,1)S(1)}, bf16[24,3072]{1,0:T(8,128)(2,1)S(1)}, u32[]{:S(2)}, u32[]{:S(2)}) collective-permute-start(bf16[24,3072]{1,0:T(8,128)(2,1)S(1)} %collective-permute-done.4), channel_id=1, source_target_pairs={{0,1},{1,2},{2,3},{3,4},{4,5},{5,6},{6,7},{7,0},{8,9},{9,10},{10,1... | collective-permute-start | bytes 442376 | tf_op jit(solution)/shard_map/ppermute | solution.py:23
  600.0 14.2 %collective-permute-start.15 = (bf16[24,6144]{1,0:T(8,128)(2,1)}, bf16[24,6144]{1,0:T(8,128)(2,1)S(1)}, u32[]{:S(2)}, u32[]{:S(2)}) collective-permute-start(bf16[24,6144]{1,0:T(8,128)(2,1)} %reduce-scatter.8.cloned.1.call-done), channel_id=1, source_target_pairs={{0,7},{1,0},{2,1},{3,2},{4,3},{5,4},{6,5},{7,6},{8,15},{9,8},{10,9... | collective-permute-start | bytes 884744 | tf_op jit(solution)/shard_map/ppermute | solution.py:26
  603.1 16.7 %collective-permute-start.14 = (bf16[24,6144]{1,0:T(8,128)(2,1)}, bf16[24,6144]{1,0:T(8,128)(2,1)S(1)}, u32[]{:S(2)}, u32[]{:S(2)}) collective-permute-start(bf16[24,6144]{1,0:T(8,128)(2,1)} %reduce-scatter.8.cloned.1.call-done), channel_id=1, source_target_pairs={{0,1},{1,2},{2,3},{3,4},{4,5},{5,6},{6,7},{7,0},{8,9},{9,10},{10,1... | collective-permute-start | bytes 884744 | tf_op jit(solution)/shard_map/ppermute | solution.py:23
  614.2 8.1 %collective-permute-start.17 = (bf16[24,6144]{1,0:T(8,128)(2,1)S(1)}, bf16[24,6144]{1,0:T(8,128)(2,1)S(1)}, u32[]{:S(2)}, u32[]{:S(2)}) collective-permute-start(bf16[24,6144]{1,0:T(8,128)(2,1)S(1)} %collective-permute-done.15), channel_id=1, source_target_pairs={{0,7},{1,0},{2,1},{3,2},{4,3},{5,4},{6,5},{7,6},{8,15},{9,8},{10,9... | collective-permute-start | bytes 884744 | tf_op jit(solution)/shard_map/ppermute | solution.py:26
  619.9 15.1 %collective-permute-start.16 = (bf16[24,6144]{1,0:T(8,128)(2,1)S(1)}, bf16[24,6144]{1,0:T(8,128)(2,1)S(1)}, u32[]{:S(2)}, u32[]{:S(2)}) collective-permute-start(bf16[24,6144]{1,0:T(8,128)(2,1)S(1)} %collective-permute-done.14), channel_id=1, source_target_pairs={{0,1},{1,2},{2,3},{3,4},{4,5},{5,6},{6,7},{7,0},{8,9},{9,10},{10,1... | collective-permute-start | bytes 884744 | tf_op jit(solution)/shard_map/ppermute | solution.py:23
  622.3 23.5 %collective-permute-start.19 = (bf16[24,6144]{1,0:T(8,128)(2,1)S(1)}, bf16[24,6144]{1,0:T(8,128)(2,1)S(1)}, u32[]{:S(2)}, u32[]{:S(2)}) collective-permute-start(bf16[24,6144]{1,0:T(8,128)(2,1)S(1)} %collective-permute-done.17), channel_id=1, source_target_pairs={{0,7},{1,0},{2,1},{3,2},{4,3},{5,4},{6,5},{7,6},{8,15},{9,8},{10,9... | collective-permute-start | bytes 884744 | tf_op jit(solution)/shard_map/ppermute | solution.py:26
  635.0 10.8 %collective-permute-start.18 = (bf16[24,6144]{1,0:T(8,128)(2,1)S(1)}, bf16[24,6144]{1,0:T(8,128)(2,1)S(1)}, u32[]{:S(2)}, u32[]{:S(2)}) collective-permute-start(bf16[24,6144]{1,0:T(8,128)(2,1)S(1)} %collective-permute-done.16), channel_id=1, source_target_pairs={{0,1},{1,2},{2,3},{3,4},{4,5},{5,6},{6,7},{7,0},{8,9},{9,10},{10,1... | collective-permute-start | bytes 884744 | tf_op jit(solution)/shard_map/ppermute | solution.py:23
  645.8 9.9 %collective-permute-start.20 = (bf16[24,6144]{1,0:T(8,128)(2,1)S(1)}, bf16[24,6144]{1,0:T(8,128)(2,1)S(1)}, u32[]{:S(2)}, u32[]{:S(2)}) collective-permute-start(bf16[24,6144]{1,0:T(8,128)(2,1)S(1)} %collective-permute-done.18), channel_id=1, source_target_pairs={{0,1},{1,2},{2,3},{3,4},{4,5},{5,6},{6,7},{7,0},{8,9},{9,10},{10,1... | collective-permute-start | bytes 884744 | tf_op jit(solution)/shard_map/ppermute | solution.py:23
  (70 other events, 366.8 us)
Sparse Core Ops, SparseCore 0:
  10.2 33.7 all-gather.4
  46.1 44.1 all-gather.6
  91.8 64.2 all-gather.8
  239.4 107.8 reduce-scatter.9
  352.6 106.4 reduce-scatter.5
  464.8 135.1 reduce-scatter.7
